TPU v7x, 32 devices: a whole 2x2x4 slice. The times are simulated.
32 devices in a mesh: groups: 2 (over y), tensor: 4 (over x, core), dp: 4 (over z).
Axes of the slice: x: 2, y: 2, z: 4, core: 2. Of those that a mesh axis runs over, the one named last changes fastest.
Arguments:
- tokens: bfloat16 [65536, 4096], P(('groups', 'dp'), 'tensor'), parts along dimension 0, may hold values from -6 to 6
- cotangent: bfloat16 [65536, 4096], P(('groups', 'dp'), 'tensor'), parts along dimension 0, may hold values from -6 to 6
- w_first: bfloat16 [16, 256, 256], P('tensor'), may hold values from -0.375 to 0.375
- w_second: bfloat16 [16, 256, 256], P('tensor'), may hold values from -0.375 to 0.375
Outputs:
- grad_tokens: bfloat16 [65536, 4096], P(('groups', 'dp'), 'tensor'), parts along dimension 0
- grad_first: float32 [32, 256, 256], P(('groups', 'tensor'), 'dp'), parts along dimension 0
- grad_second: float32 [32, 256, 256], P(('groups', 'tensor'), 'dp'), parts along dimension 0
There are 2 independent parts, one for each index of `groups`. A program takes and returns all parts, laid end to end along the dimension named above; an argument that names none is the same for every part. Nothing has to cross between parts.
All inputs are finite; a program needn't handle non-finite values.
Results may differ from a plain program's by a relative error of at most 0.0065.
Values may be sent and summed in bfloat16 or wider, within the bound.
No kernel may reach another device: no remote copies, remote signals or barrier semaphores. Data moves between devices by JAX's collectives and lax.ppermute only.
A program may use at most 192 MiB of HBM per device.

v0:
```python
import math
import jax
import jax.numpy as jnp
from jax import lax
from jax.sharding import PartitionSpec as P

NB = 16


def shards(tokens, cotangent, w_first, w_second):
    tok_rows = tokens.shape[0]
    blk_local = w_first.shape[0]
    blk_width = w_first.shape[1]
    sub_width = blk_width // NB
    dp_count = lax.axis_size("dp")
    grad_scale = 1.0 / math.sqrt(tok_rows * dp_count)
    inputs = tokens.reshape(tok_rows, blk_local, blk_width)
    upstream = cotangent.reshape(tok_rows, blk_local, blk_width)
    hidden = jnp.einsum("tbi,bij->bjt", inputs, w_first, preferred_element_type=jnp.float32).astype(
        jnp.bfloat16
    )
    hidden = hidden.reshape(blk_local, NB, sub_width, tok_rows)
    second_view = w_second.reshape(blk_local, sub_width, NB, blk_width)
    moved = lax.all_to_all(hidden, "tensor", split_axis=1, concat_axis=0, tiled=True)
    active = jnp.maximum(moved, jnp.zeros((), jnp.bfloat16))
    second_term = jnp.einsum("bcjt,tco->cjbo", active, upstream, preferred_element_type=jnp.float32)
    second_term = second_term.reshape(blk_local, blk_width, blk_width) * grad_scale
    backed = jnp.einsum("tco,cjbo->bcjt", upstream, second_view, preferred_element_type=jnp.float32)
    masked = jnp.where(moved > 0, backed, jnp.zeros((), jnp.float32)).astype(jnp.bfloat16)
    returned = lax.all_to_all(masked, "tensor", split_axis=0, concat_axis=1, tiled=True)
    returned = returned.reshape(blk_local, blk_width, tok_rows)
    first_term = (
        jnp.einsum("tbi,bjt->bij", inputs, returned, preferred_element_type=jnp.float32)
        * grad_scale
    )
    grad_tokens = jnp.einsum("bjt,bij->tbi", returned, w_first, preferred_element_type=jnp.float32)
    grad_tokens = grad_tokens.astype(jnp.bfloat16).reshape(tok_rows, blk_local * blk_width)
    grad_first, grad_second = (
        lax.psum_scatter(first_term, "dp", scatter_dimension=1, tiled=True),
        lax.psum_scatter(second_term, "dp", scatter_dimension=1, tiled=True),
    )
    return (grad_tokens, grad_first, grad_second)


def solution(mesh):
    return jax.shard_map(
        shards,
        mesh=mesh,
        in_specs=(
            P(("groups", "dp"), "tensor"),
            P(("groups", "dp"), "tensor"),
            P("tensor", None, None),
            P("tensor", None, None),
        ),
        out_specs=(
            P(("groups", "dp"), "tensor"),
            P(("groups", "tensor"), "dp", None),
            P(("groups", "tensor"), "dp", None),
        ),
        check_vma=False,
    )
```

profile of v0, /device:TPU:0, one launch (start us, length us, event | category | flops | bytes accessed | tf_op | source)
XLA Modules:
  0.0 638.0 jit_solution(12787721479795042683)
XLA Ops:
  7.2 0.0 copy-start
  7.2 1.0 copy-done
  8.2 20.5 %fusion.5 = bf16[4,256,8192]{2,1,0:T(8,128)(2,1)} fusion(bf16[4,256,256]{2,1,0:T(8,128)(2,1)S(1)} %copy-done, bf16[1024,4,8,256]{3,2,1,0:T(8,128)(2,1)} %bitcast.56), kind=kOutput, calls=%fused_computation.7 | convolution fusion | flops 4303355904 | bytes 34078720 | tf_op jit(solution)/shard_map/tbi,bij->bjt/dot_general | solution.py:19
  28.8 13.9 %copy.30 = bf16[4,16,16,8192]{3,2,0,1:T(8,128)(2,1)} copy(bf16[4,16,16,8192]{3,2,1,0:T(8,128)(2,1)} %bitcast.53) | data formatting | bytes 33554432 | tf_op jit(solution)/shard_map/reshape | solution.py:22
  42.6 7.0 %all-to-all-start = ((bf16[4,16,16,8192]{3,2,0,1:T(8,128)(2,1)}), bf16[4,16,16,8192]{3,2,0,1:T(8,128)(2,1)}, u32[]{:S(2)}, u32[]{:S(2)}) async-start(bf16[4,16,16,8192]{3,2,0,1:T(8,128)(2,1)} %copy.30), calls=%async_computation | async-start | bytes 33554432 | tf_op jit(solution)/shard_map/all_to_all | solution.py:24
  49.6 27.9 %reshape.39 = bf16[8192,4,256]{2,1,0:T(4,128)(2,1)} reshape(bf16[8192,1024]{1,0:T(8,128)(2,1)} %param.5) | data formatting | bytes 33554432 | tf_op jit(solution)/shard_map/reshape | solution.py:18
  77.5 155.8 %all-to-all-done = bf16[4,16,16,8192]{3,2,0,1:T(8,128)(2,1)} async-done(((bf16[4,16,16,8192]{3,2,0,1:T(8,128)(2,1)}), bf16[4,16,16,8192]{3,2,0,1:T(8,128)(2,1)}, u32[]{:S(2)}, u32[]{:S(2)}) %all-to-all-start) | async-done | bytes 16777248 | tf_op jit(solution)/shard_map/all_to_all | solution.py:24
  233.3 7.4 %broadcast_compare_fusion = pred[4,16,16,8192]{3,2,0,1:T(8,128)(4,1)S(1)} fusion(bf16[4,16,16,8192]{3,2,0,1:T(8,128)(2,1)} %all-to-all-done), kind=kLoop, calls=%fused_computation.15 | loop fusion | flops 8388608 | bytes 25165824 | tf_op jit(solution)/shard_map/gt | solution.py:29
  240.7 0.0 copy-start.1
  240.7 25.3 %copy.71 = pred[4,4,4,16,8192]{4,0,1,3,2:T(4,128)(4,1)} copy(pred[4,4,4,16,8192]{4,3,0,2,1:T(8,128)(4,1)S(1)} %bitcast.54) | data formatting | bytes 16777216 | tf_op jit(solution)/shard_map/gt | solution.py:29
  265.9 20.9 %gt.15 = pred[16,4,16,8192]{3,0,2,1:T(8,128)(4,1)} reshape(pred[4,4,4,16,8192]{4,1,0,3,2:T(4,128)(4,1)} %bitcast.55) | data formatting | bytes 16777216 | tf_op jit(solution)/shard_map/gt | solution.py:29
  286.8 0.0 copy-done.1
  286.8 24.9 %fusion = bf16[16,4,16,8192]{3,0,2,1:T(8,128)(2,1)} fusion(pred[16,4,16,8192]{3,0,2,1:T(8,128)(4,1)} %gt.15, bf16[4,16,16,256]{3,2,1,0:T(8,128)(2,1)S(1)} %bitcast.62, bf16[8192,4,256,1]{2,1,0,3:T(4,128)(2,1)} %bitcast.58), kind=kOutput, calls=%fused_computation.1 | convolution fusion | flops 4311744512 | bytes 42467328 | tf_op jit(solution)/shard_map/tco,cjbo->bcjt/dot_general | solution.py:28
  311.7 18.5 %copy.33 = bf16[16,4,16,8192]{3,2,1,0:T(8,128)(2,1)} copy(bf16[16,4,16,8192]{3,0,2,1:T(8,128)(2,1)} %fusion) | data formatting | bytes 33554432 | tf_op jit(solution)/shard_map/convert_element_type | solution.py:29
  330.1 7.1 %all-to-all-start.1 = ((bf16[16,4,16,8192]{3,2,1,0:T(8,128)(2,1)}), bf16[16,4,16,8192]{3,2,1,0:T(8,128)(2,1)}, u32[]{:S(2)}, u32[]{:S(2)}) async-start(bf16[16,4,16,8192]{3,2,1,0:T(8,128)(2,1)} %copy.33), calls=%async_computation.1 | async-start | bytes 33554432 | tf_op jit(solution)/shard_map/all_to_all | solution.py:30
  337.2 0.2 all-reduce.3.cloned.1.call-start
  337.5 8.0 %broadcast_maximum_fusion = bf16[4,16,16,8192]{3,2,0,1:T(8,128)(2,1)S(1)} fusion(bf16[4,16,16,8192]{3,2,0,1:T(8,128)(2,1)} %all-to-all-done), kind=kLoop, calls=%fused_computation.14 | loop fusion | flops 8388608 | bytes 33554432 | tf_op jit(solution)/shard_map/max | solution.py:25
  345.4 6.6 %copy.37 = bf16[4,4,4,16,8192]{4,3,0,1,2:T(8,128)(2,1)} copy(bf16[4,4,4,16,8192]{4,3,0,2,1:T(8,128)(2,1)S(1)} %bitcast.51) | data formatting | bytes 33554432 | tf_op jit(solution)/shard_map/max | solution.py:25
  352.0 168.3 %all-to-all-done.1 = bf16[16,4,16,8192]{3,2,1,0:T(8,128)(2,1)} async-done(((bf16[16,4,16,8192]{3,2,1,0:T(8,128)(2,1)}), bf16[16,4,16,8192]{3,2,1,0:T(8,128)(2,1)}, u32[]{:S(2)}, u32[]{:S(2)}) %all-to-all-start.1) | async-done | bytes 16777248 | tf_op jit(solution)/shard_map/all_to_all | solution.py:30
  520.3 13.9 %copy.34 = bf16[4,4,4,16,8192]{4,3,2,0,1:T(8,128)(2,1)} copy(bf16[4,4,4,16,8192]{4,3,2,1,0:T(8,128)(2,1)} %bitcast.6) | data formatting | bytes 33554432 | tf_op jit(solution)/shard_map/all_to_all | solution.py:30
  534.2 12.9 %fusion.22 = f32[4,256,256]{1,2,0:T(8,128)S(1)} fusion(bf16[4,256,8192]{2,1,0:T(8,128)(2,1)} %bitcast.49, bf16[1024,4,8,256]{3,2,1,0:T(8,128)(2,1)} %bitcast.57), kind=kOutput, calls=%fused_computation.19 | convolution fusion | flops 4295229440 | bytes 34603008 | tf_op jit(solution)/shard_map/tbi,bjt->bij/dot_general | solution.py:33
  547.1 1.4 copy.36
  548.5 0.0 all-reduce.3.cloned.1.call-update
  548.5 0.0 reduce-scatter.2.cloned.1.call-start
  548.6 0.0 copy-start.2
  548.6 13.1 %fusion.16 = f32[4,16,16,256]{3,1,2,0:T(8,128)S(1)} fusion(bf16[16,4,16,8192]{3,2,0,1:T(8,128)(2,1)} %bitcast.60, bf16[8192,4,256,1]{2,1,0,3:T(4,128)(2,1)} %bitcast.59), kind=kOutput, calls=%fused_computation.17 | convolution fusion | flops 4295229440 | bytes 34603008 | tf_op jit(solution)/shard_map/bcjt,tco->cjbo/dot_general | solution.py:26
  561.7 1.6 copy.39
  563.3 0.0 reduce-scatter.2.cloned.1.call-update
  563.3 0.0 copy-done.2
  563.4 0.6 dynamic-slice
  564.6 13.9 %convolution_convert_fusion = bf16[4,8192,256]{1,2,0:T(8,128)(2,1)} fusion(bf16[4,256,256]{2,1,0:T(8,128)(2,1)S(1)} %copy-done, bf16[4,256,8192]{2,1,0:T(8,128)(2,1)} %bitcast.50), kind=kOutput, calls=%fused_computation.8 | convolution fusion | flops 4303355904 | bytes 34078720 | tf_op jit(solution)/shard_map/bjt,bij->tbi/dot_general | solution.py:36
  578.5 22.5 %copy.40 = bf16[8192,1024]{1,0:T(8,128)(2,1)} copy(bf16[8192,1024]{0,1:T(8,128)(2,1)} %bitcast.52) | data formatting | bytes 33554432
  601.0 0.7 all-reduce.3.cloned.1.call-done
  601.7 1.0 constant_dynamic-slice_fusion
  602.6 0.8 copy.41
  603.4 27.8 %reduce-scatter.2.cloned.1.call-done = f32[4,64,256]{2,1,0:T(8,128)} async-done(((f32[4,256,256]{2,1,0:T(8,128)}), f32[4,64,256]{2,1,0:T(8,128)}) %reduce-scatter.2.cloned.1.call-update) | async-done | bytes 262160 | tf_op jit(solution)/shard_map/reduce_scatter | solution.py:40
Async XLA Ops:
  7.2 1.0 copy-start
  42.6 190.6 %all-to-all-start = ((bf16[4,16,16,8192]{3,2,0,1:T(8,128)(2,1)}), bf16[4,16,16,8192]{3,2,0,1:T(8,128)(2,1)}, u32[]{:S(2)}, u32[]{:S(2)}) async-start(bf16[4,16,16,8192]{3,2,0,1:T(8,128)(2,1)} %copy.30), calls=%async_computation | async-start | bytes 33554432 | tf_op jit(solution)/shard_map/all_to_all | solution.py:24
  240.7 46.1 %copy-start.1 = (bf16[4,256,256]{2,1,0:T(8,128)(2,1)S(1)}, bf16[4,256,256]{2,1,0:T(8,128)(2,1)}, u32[]{:S(2)}) copy-start(bf16[4,256,256]{2,1,0:T(8,128)(2,1)} %param.7) | copy-start | bytes 1572868
  330.1 190.2 %all-to-all-start.1 = ((bf16[16,4,16,8192]{3,2,1,0:T(8,128)(2,1)}), bf16[16,4,16,8192]{3,2,1,0:T(8,128)(2,1)}, u32[]{:S(2)}, u32[]{:S(2)}) async-start(bf16[16,4,16,8192]{3,2,1,0:T(8,128)(2,1)} %copy.33), calls=%async_computation.1 | async-start | bytes 33554432 | tf_op jit(solution)/shard_map/all_to_all | solution.py:30
  337.2 264.4 %all-reduce.3.cloned.1.call-start = ((), (), s32[]{:S(2)}) async-start(), calls=%async_computation.4 | async-start | bytes 2097152
  548.5 82.6 %reduce-scatter.2.cloned.1.call-start = ((), (), s32[]{:S(2)}) async-start(), calls=%async_computation.3 | async-start | bytes 1310720 | tf_op jit(solution)/shard_map/reduce_scatter | solution.py:40
  548.6 14.8 %copy-start.2 = (u32[32]{0:T(128)S(1)}, u32[32]{0:T(128)}, u32[]{:S(2)}) copy-start(u32[32]{0:T(128)} %constant.8) | copy-start | bytes 388
Sparse Core Ops, SparseCore 0:
  548.6 52.9 all-reduce.2
  604.6 26.5 reduce-scatter.1
where the time goes:
time: 641 us; the launch traced here: 638 us
  waiting for transfers between devices  353 us (55%)
  local copies, waits for them, and re-layouts  156 us (24%)
  matrix products  85.4 us (13%)
  other arithmetic  15.3 us (2%)
  between operations  14.8 us (2%)
  starting transfers between devices  14.3 us (2%)
    all_to_all x1, waiting for transfers between devices, shards(): lax.all_to_all(masked, 'tensor', split_axis=0, concat_axis=1, tiled=True)  168 us
    all_to_all x1, waiting for transfers between devices, shards(): lax.all_to_all(hidden, 'tensor', split_axis=1, concat_axis=0, tiled=True)  156 us
    gt x2, local copies, waits for them, and re-layouts, shards(): moved > 0  46.1 us
    reshape x1, local copies, waits for them, and re-layouts, shards(): upstream = cotangent.reshape(tok_rows, blk_local, blk_width)  27.9 us
    reduce_scatter x1, waiting for transfers between devices, shards(): lax.psum_scatter(second_term, 'dp', scatter_dimension=1, tiled=True)  27.8 us
    unnamed x10, local copies, waits for them, and re-layouts  25.8 us
    dot_general x1, matrix products, shards(): jnp.einsum('tco,cjbo->bcjt', upstream, second_view, preferred_element_typ...  24.9 us
    dot_general x1, matrix products, shards(): jnp.einsum('tbi,bij->bjt', inputs, w_first, preferred_element_type=jnp.fl...  20.5 us
  transfers between devices with their start and end apart: 4, of which 4 were waited for; matrix products, arithmetic and copies ran while one was open for 15% of the time, Pallas kernels for 0%

commit v1 on v0

--- a/solution.py
+++ b/solution.py
@@ -21,7 +21,19 @@
     )
     hidden = hidden.reshape(blk_local, NB, sub_width, tok_rows)
     second_view = w_second.reshape(blk_local, sub_width, NB, blk_width)
-    moved = lax.all_to_all(hidden, "tensor", split_axis=1, concat_axis=0, tiled=True)
+    ways, here = (lax.axis_size("tensor"), lax.axis_index("tensor"))
+    width = hidden.shape[1] // ways
+    lengths = list(hidden.shape)
+    lengths[1] = width
+    height = lengths[0]
+    lengths[0] = height * ways
+    full = jnp.zeros(lengths, hidden.dtype)
+    for mask in range(ways):
+        part = lax.dynamic_slice_in_dim(hidden, (here ^ mask) * width, width, axis=1)
+        if mask:
+            part = lax.ppermute(part, "tensor", [(d, d ^ mask) for d in range(ways)])
+        full = lax.dynamic_update_slice_in_dim(full, part, (here ^ mask) * height, axis=0)
+    moved = full
     active = jnp.maximum(moved, jnp.zeros((), jnp.bfloat16))
     second_term = jnp.einsum("bcjt,tco->cjbo", active, upstream, preferred_element_type=jnp.float32)
     second_term = second_term.reshape(blk_local, blk_width, blk_width) * grad_scale

time: 641 us -> 582 us (0.908)
  waiting for transfers between devices: 353 us -> 149 us
  blocking collectives: 0 us -> 186 us
  local copies, waits for them, and re-layouts: 156 us -> 135 us
  other arithmetic: 15.3 us -> 0 us
  starting transfers between devices: 14.3 us -> 3.14 us
    all_to_all x2 -> x0, waiting for transfers between devices: 324 us -> none  [the longest x1 168 us: shards(): lax.all_to_all(masked, 'tensor', split_axis=0, concat_axis=1, tiled=True)]
    all_to_all x0 -> x1, blocking collectives: none -> 186 us  [shards(): lax.all_to_all(masked, 'tensor', split_axis=0, concat_axis=1, tiled=True)]
    ppermute x0 -> x3, waiting for transfers between devices: none -> 121 us  [shards(): part = lax.ppermute(part, 'tensor', [(d, d ^ mask) for d in range(ways)])]
    gt x2 -> x0, local copies, waits for them, and re-layouts: 46.1 us -> none  [shards(): moved > 0]
    dynamic_update_slice x0 -> x4, local copies, waits for them, and re-layouts: none -> 27.2 us  [shards(): lax.dynamic_update_slice_in_dim(full, part, (here ^ mask) * height, axis=0)]
    unnamed x10 -> x15, local copies, waits for them, and re-layouts: 25.8 us -> 41.4 us
    all_to_all x2 -> x0, starting transfers between devices: 14.1 us -> none  [the longest x1 7.09 us: shards(): lax.all_to_all(masked, 'tensor', split_axis=0, concat_axis=1, tiled=True)]
    reshape x1 -> x0, local copies, waits for them, and re-layouts: 13.9 us -> none  [shards(): hidden = hidden.reshape(blk_local, NB, sub_width, tok_rows)]
  transfers between devices with their start and end apart: 4 -> 5, of which waited for: 4 -> 4; matrix products, arithmetic and copies ran while one was open for 15% -> 21% of each run, Pallas kernels for 0% -> 0%
where the time goes in v1:
time: 582 us; the launch traced here: 578 us
  blocking collectives  186 us (32%)
  waiting for transfers between devices  149 us (26%)
  local copies, waits for them, and re-layouts  135 us (23%)
  matrix products  89.7 us (15%)
  between operations  15 us (3%)
    all_to_all x1, blocking collectives, shards(): lax.all_to_all(masked, 'tensor', split_axis=0, concat_axis=1, tiled=True)  186 us
    ppermute x3, waiting for transfers between devices, shards(): part = lax.ppermute(part, 'tensor', [(d, d ^ mask) for d in range(ways)])  121 us
    unnamed x15, local copies, waits for them, and re-layouts  41.4 us
    reshape x1, local copies, waits for them, and re-layouts, shards(): upstream = cotangent.reshape(tok_rows, blk_local, blk_width)  27.9 us
    reduce_scatter x1, waiting for transfers between devices, shards(): lax.psum_scatter(second_term, 'dp', scatter_dimension=1, tiled=True)  27.8 us
    dot_general x1, matrix products, shards(): jnp.einsum('tco,cjbo->bcjt', upstream, second_view, preferred_element_typ...  27.7 us
    dynamic_update_slice x4, local copies, waits for them, and re-layouts, shards(): lax.dynamic_update_slice_in_dim(full, part, (here ^ mask) * height, axis=0)  27.2 us
    dot_general x1, matrix products, shards(): jnp.einsum('tbi,bij->bjt', inputs, w_first, preferred_element_type=jnp.fl...  20.6 us
  transfers between devices with their start and end apart: 5, of which 4 were waited for; matrix products, arithmetic and copies ran while one was open for 21% of the time, Pallas kernels for 0%

profile of v1, /device:TPU:0, one launch (start us, length us, event | category | flops | bytes accessed | tf_op | source)
XLA Modules:
  0.0 578.0 jit_solution(16631760199659432552)
XLA Ops:
  7.2 0.0 copy-start
  7.2 0.0 all-reduce.3.cloned.1.call-start
  7.2 1.0 copy-done
  8.2 20.6 %fusion.7 = bf16[4,256,8192]{2,1,0:T(8,128)(2,1)} fusion(bf16[4,256,256]{2,1,0:T(8,128)(2,1)S(1)} %copy-done, bf16[1024,4,8,256]{3,2,1,0:T(8,128)(2,1)} %bitcast.43), kind=kOutput, calls=%fused_computation.8 | convolution fusion | flops 4303355904 | bytes 34078720 | tf_op jit(solution)/shard_map/tbi,bij->bjt/dot_general | solution.py:19
  28.8 8.8 %constant_dynamic-slice_fusion = (bf16[4,4,16,8192]{3,2,1,0:T(8,128)(2,1)S(1)}, bf16[4,4,16,8192]{3,2,1,0:T(8,128)(2,1)S(1)}, bf16[4,4,16,8192]{3,2,1,0:T(8,128)(2,1)S(1)}, bf16[4,4,16,8192]{3,2,1,0:T(8,128)(2,1)}) fusion(bf16[4,16,16,8192]{3,2,1,0:T(8,128)(2,1)} %bitcast.40, s32[]{:T(128)S(6)} %select_n.23, s32[]{:T(128)S(6)} %select_n.22, ...), kind=kLoop, calls=%fused_computation.20 | loop fusion | bytes 33554448 | tf_op jit(solution)/shard_map/dynamic_slice | solution.py:32
  37.7 5.2 copy.56
  42.9 0.5 collective-permute-start
  43.4 5.2 copy.57
  48.6 2.5 collective-permute-start.1
  51.0 5.2 copy.58
  56.3 0.1 collective-permute-start.2
  56.4 27.9 %reshape.31 = bf16[8192,4,256]{2,1,0:T(4,128)(2,1)} reshape(bf16[8192,1024]{1,0:T(8,128)(2,1)} %param.5) | data formatting | bytes 33554432 | tf_op jit(solution)/shard_map/reshape | solution.py:18
  84.3 0.0 copy-start.1
  84.3 7.2 %broadcast.13 = bf16[16,4,16,8192]{3,0,2,1:T(8,128)(2,1)} broadcast(bf16[]{:T(256)} %constant.2.clone.1), dimensions={} | broadcast | bytes 16777218 | tf_op jit(solution)/shard_map/broadcast.3
  91.4 0.0 copy-done.1
  91.5 0.0 copy-start.2
  91.5 5.3 copy_dynamic-update-slice_fusion
  96.7 0.0 collective-permute-done
  96.7 7.3 %constant_dynamic-update-slice_fusion.2 = bf16[16,4,16,8192]{3,0,2,1:T(8,128)(2,1)} fusion(bf16[16,4,16,8192]{3,0,2,1:T(8,128)(2,1)} %copy_dynamic-update-slice_fusion, bf16[4,4,16,8192]{3,0,2,1:T(4,128)(2,1)} %collective-permute-done, s32[]{:T(128)S(6)} %select_n.21), kind=kLoop, calls=%fused_computation.23 | loop fusion | bytes 8388612 | tf_op jit(solution)/shard_map/dynamic_update_slice | solution.py:35
  104.1 38.7 %collective-permute-done.1 = bf16[4,4,16,8192]{3,0,2,1:T(4,128)(2,1)} collective-permute-done((bf16[4,4,16,8192]{3,0,2,1:T(4,128)(2,1)}, bf16[4,4,16,8192]{3,0,2,1:T(4,128)(2,1)}, u32[]{:S(2)}, u32[]{:S(2)}) %collective-permute-start.1) | collective-permute-done | bytes 4194336 | tf_op jit(solution)/shard_map/ppermute | solution.py:34
  142.8 7.3 %constant_dynamic-update-slice_fusion.1 = bf16[16,4,16,8192]{3,0,2,1:T(8,128)(2,1)} fusion(bf16[16,4,16,8192]{3,0,2,1:T(8,128)(2,1)} %constant_dynamic-update-slice_fusion.2, bf16[4,4,16,8192]{3,0,2,1:T(4,128)(2,1)} %collective-permute-done.1, s32[]{:T(128)S(6)} %select_n.22), kind=kLoop, calls=%fused_computation.21 | loop fusion | bytes 8388612 | tf_op jit(solution)/shard_map/dynamic_update_slice | solution.py:35
  150.1 82.2 %collective-permute-done.2 = bf16[4,4,16,8192]{3,0,2,1:T(4,128)(2,1)} collective-permute-done((bf16[4,4,16,8192]{3,0,2,1:T(4,128)(2,1)}, bf16[4,4,16,8192]{3,0,2,1:T(4,128)(2,1)}, u32[]{:S(2)}, u32[]{:S(2)}) %collective-permute-start.2) | collective-permute-done | bytes 4194336 | tf_op jit(solution)/shard_map/ppermute | solution.py:34
  232.3 7.3 %constant_dynamic-update-slice_fusion = bf16[16,4,16,8192]{3,0,2,1:T(8,128)(2,1)} fusion(bf16[16,4,16,8192]{3,0,2,1:T(8,128)(2,1)} %constant_dynamic-update-slice_fusion.1, bf16[4,4,16,8192]{3,0,2,1:T(4,128)(2,1)} %collective-permute-done.2, s32[]{:T(128)S(6)} %select_n.23), kind=kLoop, calls=%fused_computation.19 | loop fusion | bytes 8388612 | tf_op jit(solution)/shard_map/dynamic_update_slice | solution.py:35
  239.6 0.0 copy-done.2
  239.6 27.7 %fusion = bf16[16,4,16,8192]{3,0,2,1:T(8,128)(2,1)} fusion(bf16[16,4,16,8192]{3,0,2,1:T(8,128)(2,1)} %constant_dynamic-update-slice_fusion, bf16[4,16,16,256]{3,2,1,0:T(8,128)(2,1)S(1)} %bitcast.48, bf16[8192,4,256,1]{2,1,0,3:T(4,128)(2,1)} %bitcast.45), kind=kOutput, calls=%fused_computation.1 | convolution fusion | flops 4320133120 | bytes 50855936 | tf_op jit(solution)/shard_map/tco,cjbo->bcjt/dot_general | solution.py:40
  267.3 14.7 %copy.41 = bf16[16,4,16,8192]{3,2,1,0:T(8,128)(2,1)S(1)} copy(bf16[16,4,16,8192]{3,0,2,1:T(8,128)(2,1)} %fusion) | data formatting | bytes 33554432 | tf_op jit(solution)/shard_map/convert_element_type | solution.py:41
  282.0 186.1 %all_to_all.15 = bf16[16,4,16,8192]{3,2,1,0:T(8,128)(2,1)S(1)} all-to-all(bf16[16,4,16,8192]{3,2,1,0:T(8,128)(2,1)S(1)} %copy.41), channel_id=1, replica_groups=mesh['groups'=2,'tensor'=4,'dp'=4] {'tensor'}, dimensions={0} | all-to-all | bytes 33554432 | tf_op jit(solution)/shard_map/all_to_all | solution.py:42
  468.2 6.5 %copy.42 = bf16[4,4,4,16,8192]{4,3,2,0,1:T(8,128)(2,1)} copy(bf16[4,4,4,16,8192]{4,3,2,1,0:T(8,128)(2,1)S(1)} %bitcast.41) | data formatting | bytes 33554432 | tf_op jit(solution)/shard_map/all_to_all | solution.py:42
  474.7 12.9 %fusion.18 = f32[4,256,256]{1,2,0:T(8,128)S(1)} fusion(bf16[4,256,8192]{2,1,0:T(8,128)(2,1)} %bitcast.38, bf16[1024,4,8,256]{3,2,1,0:T(8,128)(2,1)} %bitcast.44), kind=kOutput, calls=%fused_computation.17 | convolution fusion | flops 4295229440 | bytes 34603008 | tf_op jit(solution)/shard_map/tbi,bjt->bij/dot_general | solution.py:45
  487.6 1.4 copy.44
  489.0 0.0 all-reduce.3.cloned.1.call-update
  489.0 0.0 copy-start.3
  489.0 0.0 reduce-scatter.2.cloned.1.call-start
  489.1 14.5 %fusion.21 = f32[4,16,16,256]{3,1,2,0:T(8,128)} fusion(bf16[8192,4,256,1]{2,1,0,3:T(4,128)(2,1)} %bitcast.46, bf16[16,4,16,8192]{3,0,2,1:T(8,128)(2,1)} %constant_dynamic-update-slice_fusion), kind=kOutput, calls=%fused_computation.18 | convolution fusion | flops 4303618048 | bytes 34603008 | tf_op jit(solution)/shard_map/bcjt,tco->cjbo/dot_general | solution.py:38
  503.6 0.0 reduce-scatter.2.cloned.1.call-update
  503.6 0.0 copy-done.3
  503.6 0.6 dynamic-slice
  504.9 13.9 %convolution_convert_fusion = bf16[4,8192,256]{1,2,0:T(8,128)(2,1)} fusion(bf16[4,256,256]{2,1,0:T(8,128)(2,1)S(1)} %copy-done, bf16[4,256,8192]{2,1,0:T(8,128)(2,1)} %bitcast.39), kind=kOutput, calls=%fused_computation.9 | convolution fusion | flops 4303355904 | bytes 34078720 | tf_op jit(solution)/shard_map/bjt,bij->tbi/dot_general | solution.py:48
  518.8 22.5 %copy.46 = bf16[8192,1024]{1,0:T(8,128)(2,1)} copy(bf16[8192,1024]{0,1:T(8,128)(2,1)} %bitcast.42) | data formatting | bytes 33554432
  541.3 0.1 all-reduce.3.cloned.1.call-done
  541.4 1.0 constant_dynamic-slice_fusion.4
  542.3 0.8 copy.47
  543.1 27.8 %reduce-scatter.2.cloned.1.call-done = f32[4,64,256]{2,1,0:T(8,128)} async-done(((f32[4,256,256]{2,1,0:T(8,128)}), f32[4,64,256]{2,1,0:T(8,128)}) %reduce-scatter.2.cloned.1.call-update) | async-done | bytes 262160 | tf_op jit(solution)/shard_map/reduce_scatter | solution.py:52
Async XLA Ops:
  7.2 1.0 copy-start
  7.2 534.2 %all-reduce.3.cloned.1.call-start = ((), (), s32[]{:S(2)}) async-start(), calls=%async_computation.3 | async-start | bytes 2097152
  42.9 53.8 %collective-permute-start = (bf16[4,4,16,8192]{3,0,2,1:T(4,128)(2,1)}, bf16[4,4,16,8192]{3,0,2,1:T(4,128)(2,1)}, u32[]{:S(2)}, u32[]{:S(2)}) collective-permute-start(bf16[4,4,16,8192]{3,0,2,1:T(4,128)(2,1)} %copy.56), channel_id=1, source_target_pairs={{0,4},{4,0},{8,12},{12,8},{1,5},{5,1},{9,13},{13,9},{2,6},{6,2},{1... | collective-permute-start | bytes 12582920 | tf_op jit(solution)/shard_map/ppermute | solution.py:34
  48.6 94.2 %collective-permute-start.1 = (bf16[4,4,16,8192]{3,0,2,1:T(4,128)(2,1)}, bf16[4,4,16,8192]{3,0,2,1:T(4,128)(2,1)}, u32[]{:S(2)}, u32[]{:S(2)}) collective-permute-start(bf16[4,4,16,8192]{3,0,2,1:T(4,128)(2,1)} %copy.57), channel_id=1, source_target_pairs={{0,8},{4,12},{8,0},{12,4},{1,9},{5,13},{9,1},{13,5},{2,10},{6,14},... | collective-permute-start | bytes 12582920 | tf_op jit(solution)/shard_map/ppermute | solution.py:34
  56.3 176.0 %collective-permute-start.2 = (bf16[4,4,16,8192]{3,0,2,1:T(4,128)(2,1)}, bf16[4,4,16,8192]{3,0,2,1:T(4,128)(2,1)}, u32[]{:S(2)}, u32[]{:S(2)}) collective-permute-start(bf16[4,4,16,8192]{3,0,2,1:T(4,128)(2,1)} %copy.58), channel_id=1, source_target_pairs={{0,12},{4,8},{8,4},{12,0},{1,13},{5,9},{9,5},{13,1},{2,14},{6,10},... | collective-permute-start | bytes 12582920 | tf_op jit(solution)/shard_map/ppermute | solution.py:34
  84.3 7.2 %copy-start.1 = (bf16[4,4,16,8192]{3,2,1,0:T(8,128)(2,1)S(1)}, bf16[4,4,16,8192]{3,2,1,0:T(8,128)(2,1)}, u32[]{:S(2)}) copy-start(bf16[4,4,16,8192]{3,2,1,0:T(8,128)(2,1)} %get-tuple-element.15) | copy-start | bytes 12582916
  91.5 148.2 %copy-start.2 = (bf16[4,256,256]{2,1,0:T(8,128)(2,1)S(1)}, bf16[4,256,256]{2,1,0:T(8,128)(2,1)}, u32[]{:S(2)}) copy-start(bf16[4,256,256]{2,1,0:T(8,128)(2,1)} %param.7) | copy-start | bytes 1572868
  489.0 14.6 %copy-start.3 = (u32[32]{0:T(128)S(1)}, u32[32]{0:T(128)}, u32[]{:S(2)}) copy-start(u32[32]{0:T(128)} %constant.25) | copy-start | bytes 388
  489.0 81.9 %reduce-scatter.2.cloned.1.call-start = ((), (), s32[]{:S(2)}) async-start(), calls=%async_computation.2 | async-start | bytes 1310720 | tf_op jit(solution)/shard_map/reduce_scatter | solution.py:52
Sparse Core Ops, SparseCore 0:
  489.1 52.1 all-reduce.2
  544.3 26.5 reduce-scatter.1
